TPU v7x, 256 devices: a whole 4x4x8 slice. The times are simulated.
256 devices in a mesh: ctx: 32 (over x, z), head: 8 (over y, core).
Axes of the slice: x: 4, y: 4, z: 8, core: 2. Of those that a mesh axis runs over, the one named last changes fastest.
Arguments:
- query_in: bfloat16 [16384, 2048], P('ctx', 'head'), may hold values from -6 to 6
- key_in: bfloat16 [16384, 2048], P('ctx', 'head'), may hold values from -6 to 6
- value_in: bfloat16 [16384, 4096], P('ctx', 'head'), may hold values from -6 to 6
- query_taps: float32 [4, 2048], P(None, 'head'), may hold values from -3 to 3
- key_taps: float32 [4, 2048], P(None, 'head'), may hold values from -3 to 3
- value_taps: float32 [4, 4096], P(None, 'head'), may hold values from -3 to 3
- log_decay: float32 [32, 16384], P('head', 'ctx'), may hold values from -2 to 0
- beta_logit: float32 [32, 16384], P('head', 'ctx'), may hold values from -9 to 2
- gate_in: bfloat16 [16384, 4096], P('ctx', 'head'), may hold values from -6 to 6
- norm_gain: float32 [128], replicated, may hold values from 0.1 to 1.9
Outputs:
- core_out: bfloat16 [16384, 4096], P(('ctx', 'head'))
All inputs are finite; a program needn't handle non-finite values.
Results may differ from a plain program's by a relative error of at most 0.005.
Values may be sent and summed in bfloat16 or wider, within the bound.
No kernel may reach another device: no remote copies, remote signals or barrier semaphores. Data moves between devices by JAX's collectives and lax.ppermute only.
A program may use at most 64 MiB of HBM per device.

v0:
```python
import jax
import jax.numpy as jnp
from jax import lax
from jax.sharding import PartitionSpec as P

GROUP = 64


highest = lax.Precision.HIGHEST
norm_eps = 1e-06


def shifted(value, axis, steps):
    count = lax.axis_size(axis)
    first, last = (max(0, -steps), min(count, count - steps))
    return lax.ppermute(value, axis, [(source, source + steps) for source in range(first, last)])


def causal_conv(joined, taps, length):
    summed = jnp.zeros((length, joined.shape[1]), jnp.float32)
    for offset in range(taps.shape[0]):
        summed = summed + taps[offset] * joined[offset : offset + length].astype(jnp.float32)
    return jax.nn.silu(summed)


def unit_rows(matrix):
    return matrix * lax.rsqrt(jnp.sum(matrix * matrix, axis=-1, keepdims=True) + norm_eps)


def group_terms(query, keys, values, beta, logdecay):
    length = logdecay.shape[-1]
    cumul = jnp.cumsum(logdecay, axis=-1)
    row_ids = lax.broadcasted_iota(jnp.int32, (length, length), 0)
    col_ids = lax.broadcasted_iota(jnp.int32, (length, length), 1)
    inside = col_ids <= row_ids
    differ = cumul[..., :, None] - cumul[..., None, :]
    decay_mask = jnp.where(inside, jnp.exp(jnp.where(inside, differ, 0.0)), 0.0)
    keygram = jnp.einsum("...ik,...jk->...ij", keys, keys, precision=highest)
    strict = jnp.where(col_ids < row_ids, beta[..., :, None] * keygram * decay_mask, 0.0)
    identity_mats = jnp.broadcast_to(jnp.eye(length, dtype=jnp.float32), strict.shape)
    inverse = lax.linalg.triangular_solve(
        identity_mats + strict, identity_mats, left_side=True, lower=True, unit_diagonal=True
    )
    upd_values = jnp.einsum(
        "...ij,...jd->...id", inverse, beta[..., None] * values, precision=highest
    )
    upd_keys = jnp.einsum(
        "...ij,...jd->...id", inverse, (beta * jnp.exp(cumul))[..., None] * keys, precision=highest
    )
    scores = jnp.einsum("...ik,...jk->...ij", query, keys, precision=highest) * decay_mask
    last_log = cumul[..., -1:]
    query_decay = query * jnp.exp(cumul)[..., None]
    key_decay = keys * jnp.exp(last_log - cumul)[..., None]
    return (upd_values, upd_keys, scores, query_decay, key_decay, last_log[..., 0])


def group_step(state, terms):
    upd_values, upd_keys, scores, query_decay, key_decay, last_log = terms
    new_values = upd_values - jnp.einsum("...ik,...kd->...id", upd_keys, state, precision=highest)
    output = jnp.einsum("...ik,...kd->...id", query_decay, state, precision=highest)
    output = output + jnp.einsum("...ij,...jd->...id", scores, new_values, precision=highest)
    state = jnp.exp(last_log)[..., None, None] * state + jnp.einsum(
        "...ik,...id->...kd", key_decay, new_values, precision=highest
    )
    return (state, output)


def matmul_pair(left_mats, right_mats):
    return jnp.einsum("...ij,...jk->...ik", left_mats, right_mats, precision=highest)


def body(
    query_in,
    key_in,
    value_in,
    query_taps,
    key_taps,
    value_taps,
    log_decay,
    beta_logit,
    gate_in,
    norm_gain,
):
    head_size = norm_gain.shape[0]
    length = query_in.shape[0]
    value_heads = log_decay.shape[0]
    key_heads = query_in.shape[1] // head_size
    share_ratio = value_heads // key_heads
    rim_width = query_taps.shape[0] - 1
    groups_dev = length // GROUP
    tail_rows = shifted(
        (
            query_in[length - rim_width :],
            key_in[length - rim_width :],
            value_in[length - rim_width :],
        ),
        "ctx",
        1,
    )
    query_conv = causal_conv(jnp.concatenate([tail_rows[0], query_in], axis=0), query_taps, length)
    key_conv = causal_conv(jnp.concatenate([tail_rows[1], key_in], axis=0), key_taps, length)
    value_conv = causal_conv(jnp.concatenate([tail_rows[2], value_in], axis=0), value_taps, length)
    queries = (
        unit_rows(query_conv.reshape(length, key_heads, head_size)) * head_size ** (-0.5)
    ).astype(jnp.bfloat16)
    keys = unit_rows(key_conv.reshape(length, key_heads, head_size)).astype(jnp.bfloat16)
    values = value_conv.reshape(length, value_heads, head_size).astype(jnp.bfloat16)

    def blocked(array):
        return (
            array.astype(jnp.float32)
            .reshape(groups_dev, GROUP, array.shape[1], head_size)
            .transpose(0, 2, 1, 3)
        )

    def blocked_rates(array):
        return array.reshape(value_heads, groups_dev, GROUP).transpose(1, 0, 2)

    query_blocks = blocked(jnp.repeat(queries, share_ratio, axis=1))
    key_blocks = blocked(jnp.repeat(keys, share_ratio, axis=1))
    value_blocks = blocked(values)
    beta_blocks = blocked_rates(jax.nn.sigmoid(beta_logit))
    decay_blocks = blocked_rates(log_decay)
    terms = group_terms(query_blocks, key_blocks, value_blocks, beta_blocks, decay_blocks)
    upd_values, upd_keys, scores, query_decay, key_decay, last_log = terms
    identity_state = jnp.broadcast_to(
        jnp.eye(head_size, dtype=jnp.float32), (value_heads, head_size, head_size)
    )
    group_maps = jnp.exp(last_log)[..., None, None] * identity_state - jnp.einsum(
        "...ik,...ij->...kj", key_decay, upd_keys, precision=highest
    )
    query_effect = query_decay - matmul_pair(scores, upd_keys)

    def local_step(carry, packed):
        state, product = carry
        group, group_map = packed
        state, output = group_step(state, group)
        return ((state, matmul_pair(group_map, product)), output)

    zero_state = jnp.zeros((value_heads, head_size, head_size), jnp.float32)
    (local_state, shard_map_mat), local_out = lax.scan(
        local_step, (zero_state, identity_state), (terms, group_maps)
    )

    def chain_turn(turn, incoming_state):
        return shifted(matmul_pair(shard_map_mat, incoming_state) + local_state, "ctx", 1)

    incoming = lax.fori_loop(0, lax.axis_size("ctx") - 1, chain_turn, zero_state)

    def carried_step(state, packed):
        effect_group, group_map = packed
        return (matmul_pair(group_map, state), matmul_pair(effect_group, state))

    _, carried_out = lax.scan(carried_step, incoming, (query_effect, group_maps))
    output = (local_out + carried_out).transpose(0, 2, 1, 3).reshape(length, value_heads, head_size)
    gates = gate_in.reshape(length, value_heads, head_size).astype(jnp.float32)
    normed = (
        output
        * lax.rsqrt(jnp.mean(output * output, axis=-1, keepdims=True) + norm_eps)
        * norm_gain
        * jax.nn.silu(gates)
    )
    normed = normed.astype(jnp.bfloat16).reshape(length, value_heads * head_size)
    return lax.all_to_all(normed, "head", split_axis=0, concat_axis=1, tiled=True)


def solution(mesh):
    in_specs = (
        P("ctx", "head"),
        P("ctx", "head"),
        P("ctx", "head"),
        P(None, "head"),
        P(None, "head"),
        P(None, "head"),
        P("head", "ctx"),
        P("head", "ctx"),
        P("ctx", "head"),
        P(),
    )
    out_specs = P(("ctx", "head"), None)
    return jax.shard_map(body, mesh=mesh, in_specs=in_specs, out_specs=out_specs, check_vma=False)
```

profile of v0, /device:TPU:4, one launch (start us, length us, event | category | flops | bytes accessed | tf_op | source)
XLA Modules:
  0.0 657.1 jit_solution(1488363138327916721)
XLA Ops:
  23.5 157.3 %custom-call.3 = f32[8,4,1,64,64]{3,4,2,1,0:T(8,128)S(1)} custom-call(f32[8,4,1,64,64]{4,3,2,1,0:T(8,128)S(1)} %fusion.42), custom_call_target="InvertDiagBlocksLowerTriangular" | custom-call | tf_op jit(solution)/shard_map/triangular_solve | solution.py:41
  204.8 53.3 %while.39 = (s32[]{:T(128)}, f32[4,128,128]{2,1,0:T(8,128)S(1)}, f32[4,128,128]{2,1,0:T(8,128)S(1)}, f32[8,4,64,128]{3,2,1,0:T(8,128)S(1)}, f32[8,4]{1,0:T(8,128...) while((s32[]{:T(128)}, f32[4,128,128]{2,1,0:T(8,128)S(1)}, ...), condition=%wide.region_4.5_spmd.clone, body=%wide.region_3.4_spmd.clone.sunk | while | flops 277217280 | bytes 3804367 | solution.py:141
  258.1 357.7 %while.37 = (s32[]{:T(128)}, f32[4,128,128]{2,1,0:T(8,128)S(1)}, f32[4,128,128]{2,1,0:T(8,128)S(1)}, f32[4,128,128]{2,1,0:T(8,128)S(1)}, s32[]{:T(128)}) while((s32[]{:T(128)}, f32[4,128,128]{2,1,0:T(8,128)S(1)}, f32[4,128,128]{2,1,0:T(8,128)S(1)}, f32[4,128,128]{2,1,0:T(8,128)S(1)}, s32[]{:T(128)}) %tuple.71), condition=%wide.region_6.7_spmd, body=%wide.region_5.6_spmd.sunk | while | flops 100728832 | bytes 2097253 | solution.py:148
  283.1 8.4 %collective-permute-done = f32[4,128,128]{2,1,0:T(8,128)S(1)} collective-permute-done((f32[4,128,128]{2,1,0:T(8,128)S(1)}, f32[4,128,128]{2,1,0:T(8,128)S(1)}, u32[]{:S(2)}, u32[]{:S(2)}) %collective-permute-start) | collective-permute-done | bytes 262176 | tf_op jit(solution)/shard_map/while/body/eval_jaxpr/ppermute | solution.py:16
  304.7 8.4 %collective-permute-done = f32[4,128,128]{2,1,0:T(8,128)S(1)} collective-permute-done((f32[4,128,128]{2,1,0:T(8,128)S(1)}, f32[4,128,128]{2,1,0:T(8,128)S(1)}, u32[]{:S(2)}, u32[]{:S(2)}) %collective-permute-start) | collective-permute-done | bytes 262176 | tf_op jit(solution)/shard_map/while/body/eval_jaxpr/ppermute | solution.py:16
  315.4 9.1 %collective-permute-done = f32[4,128,128]{2,1,0:T(8,128)S(1)} collective-permute-done((f32[4,128,128]{2,1,0:T(8,128)S(1)}, f32[4,128,128]{2,1,0:T(8,128)S(1)}, u32[]{:S(2)}, u32[]{:S(2)}) %collective-permute-start) | collective-permute-done | bytes 262176 | tf_op jit(solution)/shard_map/while/body/eval_jaxpr/ppermute | solution.py:16
  326.8 10.2 %collective-permute-done = f32[4,128,128]{2,1,0:T(8,128)S(1)} collective-permute-done((f32[4,128,128]{2,1,0:T(8,128)S(1)}, f32[4,128,128]{2,1,0:T(8,128)S(1)}, u32[]{:S(2)}, u32[]{:S(2)}) %collective-permute-start) | collective-permute-done | bytes 262176 | tf_op jit(solution)/shard_map/while/body/eval_jaxpr/ppermute | solution.py:16
  339.4 11.2 %collective-permute-done = f32[4,128,128]{2,1,0:T(8,128)S(1)} collective-permute-done((f32[4,128,128]{2,1,0:T(8,128)S(1)}, f32[4,128,128]{2,1,0:T(8,128)S(1)}, u32[]{:S(2)}, u32[]{:S(2)}) %collective-permute-start) | collective-permute-done | bytes 262176 | tf_op jit(solution)/shard_map/while/body/eval_jaxpr/ppermute | solution.py:16
  352.9 10.3 %collective-permute-done = f32[4,128,128]{2,1,0:T(8,128)S(1)} collective-permute-done((f32[4,128,128]{2,1,0:T(8,128)S(1)}, f32[4,128,128]{2,1,0:T(8,128)S(1)}, u32[]{:S(2)}, u32[]{:S(2)}) %collective-permute-start) | collective-permute-done | bytes 262176 | tf_op jit(solution)/shard_map/while/body/eval_jaxpr/ppermute | solution.py:16
  365.5 9.4 %collective-permute-done = f32[4,128,128]{2,1,0:T(8,128)S(1)} collective-permute-done((f32[4,128,128]{2,1,0:T(8,128)S(1)}, f32[4,128,128]{2,1,0:T(8,128)S(1)}, u32[]{:S(2)}, u32[]{:S(2)}) %collective-permute-start) | collective-permute-done | bytes 262176 | tf_op jit(solution)/shard_map/while/body/eval_jaxpr/ppermute | solution.py:16
  377.3 8.6 %collective-permute-done = f32[4,128,128]{2,1,0:T(8,128)S(1)} collective-permute-done((f32[4,128,128]{2,1,0:T(8,128)S(1)}, f32[4,128,128]{2,1,0:T(8,128)S(1)}, u32[]{:S(2)}, u32[]{:S(2)}) %collective-permute-start) | collective-permute-done | bytes 262176 | tf_op jit(solution)/shard_map/while/body/eval_jaxpr/ppermute | solution.py:16
  388.2 8.4 %collective-permute-done = f32[4,128,128]{2,1,0:T(8,128)S(1)} collective-permute-done((f32[4,128,128]{2,1,0:T(8,128)S(1)}, f32[4,128,128]{2,1,0:T(8,128)S(1)}, u32[]{:S(2)}, u32[]{:S(2)}) %collective-permute-start) | collective-permute-done | bytes 262176 | tf_op jit(solution)/shard_map/while/body/eval_jaxpr/ppermute | solution.py:16
  399.0 8.4 %collective-permute-done = f32[4,128,128]{2,1,0:T(8,128)S(1)} collective-permute-done((f32[4,128,128]{2,1,0:T(8,128)S(1)}, f32[4,128,128]{2,1,0:T(8,128)S(1)}, u32[]{:S(2)}, u32[]{:S(2)}) %collective-permute-start) | collective-permute-done | bytes 262176 | tf_op jit(solution)/shard_map/while/body/eval_jaxpr/ppermute | solution.py:16
  409.8 8.4 %collective-permute-done = f32[4,128,128]{2,1,0:T(8,128)S(1)} collective-permute-done((f32[4,128,128]{2,1,0:T(8,128)S(1)}, f32[4,128,128]{2,1,0:T(8,128)S(1)}, u32[]{:S(2)}, u32[]{:S(2)}) %collective-permute-start) | collective-permute-done | bytes 262176 | tf_op jit(solution)/shard_map/while/body/eval_jaxpr/ppermute | solution.py:16
  420.6 8.6 %collective-permute-done = f32[4,128,128]{2,1,0:T(8,128)S(1)} collective-permute-done((f32[4,128,128]{2,1,0:T(8,128)S(1)}, f32[4,128,128]{2,1,0:T(8,128)S(1)}, u32[]{:S(2)}, u32[]{:S(2)}) %collective-permute-start) | collective-permute-done | bytes 262176 | tf_op jit(solution)/shard_map/while/body/eval_jaxpr/ppermute | solution.py:16
  431.5 9.7 %collective-permute-done = f32[4,128,128]{2,1,0:T(8,128)S(1)} collective-permute-done((f32[4,128,128]{2,1,0:T(8,128)S(1)}, f32[4,128,128]{2,1,0:T(8,128)S(1)}, u32[]{:S(2)}, u32[]{:S(2)}) %collective-permute-start) | collective-permute-done | bytes 262176 | tf_op jit(solution)/shard_map/while/body/eval_jaxpr/ppermute | solution.py:16
  443.5 10.9 %collective-permute-done = f32[4,128,128]{2,1,0:T(8,128)S(1)} collective-permute-done((f32[4,128,128]{2,1,0:T(8,128)S(1)}, f32[4,128,128]{2,1,0:T(8,128)S(1)}, u32[]{:S(2)}, u32[]{:S(2)}) %collective-permute-start) | collective-permute-done | bytes 262176 | tf_op jit(solution)/shard_map/while/body/eval_jaxpr/ppermute | solution.py:16
  456.8 10.5 %collective-permute-done = f32[4,128,128]{2,1,0:T(8,128)S(1)} collective-permute-done((f32[4,128,128]{2,1,0:T(8,128)S(1)}, f32[4,128,128]{2,1,0:T(8,128)S(1)}, u32[]{:S(2)}, u32[]{:S(2)}) %collective-permute-start) | collective-permute-done | bytes 262176 | tf_op jit(solution)/shard_map/while/body/eval_jaxpr/ppermute | solution.py:16
  469.6 9.6 %collective-permute-done = f32[4,128,128]{2,1,0:T(8,128)S(1)} collective-permute-done((f32[4,128,128]{2,1,0:T(8,128)S(1)}, f32[4,128,128]{2,1,0:T(8,128)S(1)}, u32[]{:S(2)}, u32[]{:S(2)}) %collective-permute-start) | collective-permute-done | bytes 262176 | tf_op jit(solution)/shard_map/while/body/eval_jaxpr/ppermute | solution.py:16
  481.5 8.8 %collective-permute-done = f32[4,128,128]{2,1,0:T(8,128)S(1)} collective-permute-done((f32[4,128,128]{2,1,0:T(8,128)S(1)}, f32[4,128,128]{2,1,0:T(8,128)S(1)}, u32[]{:S(2)}, u32[]{:S(2)}) %collective-permute-start) | collective-permute-done | bytes 262176 | tf_op jit(solution)/shard_map/while/body/eval_jaxpr/ppermute | solution.py:16
  492.6 8.4 %collective-permute-done = f32[4,128,128]{2,1,0:T(8,128)S(1)} collective-permute-done((f32[4,128,128]{2,1,0:T(8,128)S(1)}, f32[4,128,128]{2,1,0:T(8,128)S(1)}, u32[]{:S(2)}, u32[]{:S(2)}) %collective-permute-start) | collective-permute-done | bytes 262176 | tf_op jit(solution)/shard_map/while/body/eval_jaxpr/ppermute | solution.py:16
  503.4 8.4 %collective-permute-done = f32[4,128,128]{2,1,0:T(8,128)S(1)} collective-permute-done((f32[4,128,128]{2,1,0:T(8,128)S(1)}, f32[4,128,128]{2,1,0:T(8,128)S(1)}, u32[]{:S(2)}, u32[]{:S(2)}) %collective-permute-start) | collective-permute-done | bytes 262176 | tf_op jit(solution)/shard_map/while/body/eval_jaxpr/ppermute | solution.py:16
  514.2 8.4 %collective-permute-done = f32[4,128,128]{2,1,0:T(8,128)S(1)} collective-permute-done((f32[4,128,128]{2,1,0:T(8,128)S(1)}, f32[4,128,128]{2,1,0:T(8,128)S(1)}, u32[]{:S(2)}, u32[]{:S(2)}) %collective-permute-start) | collective-permute-done | bytes 262176 | tf_op jit(solution)/shard_map/while/body/eval_jaxpr/ppermute | solution.py:16
  525.0 8.4 %collective-permute-done = f32[4,128,128]{2,1,0:T(8,128)S(1)} collective-permute-done((f32[4,128,128]{2,1,0:T(8,128)S(1)}, f32[4,128,128]{2,1,0:T(8,128)S(1)}, u32[]{:S(2)}, u32[]{:S(2)}) %collective-permute-start) | collective-permute-done | bytes 262176 | tf_op jit(solution)/shard_map/while/body/eval_jaxpr/ppermute | solution.py:16
  535.8 9.6 %collective-permute-done = f32[4,128,128]{2,1,0:T(8,128)S(1)} collective-permute-done((f32[4,128,128]{2,1,0:T(8,128)S(1)}, f32[4,128,128]{2,1,0:T(8,128)S(1)}, u32[]{:S(2)}, u32[]{:S(2)}) %collective-permute-start) | collective-permute-done | bytes 262176 | tf_op jit(solution)/shard_map/while/body/eval_jaxpr/ppermute | solution.py:16
  547.7 10.7 %collective-permute-done = f32[4,128,128]{2,1,0:T(8,128)S(1)} collective-permute-done((f32[4,128,128]{2,1,0:T(8,128)S(1)}, f32[4,128,128]{2,1,0:T(8,128)S(1)}, u32[]{:S(2)}, u32[]{:S(2)}) %collective-permute-start) | collective-permute-done | bytes 262176 | tf_op jit(solution)/shard_map/while/body/eval_jaxpr/ppermute | solution.py:16
  560.7 10.6 %collective-permute-done = f32[4,128,128]{2,1,0:T(8,128)S(1)} collective-permute-done((f32[4,128,128]{2,1,0:T(8,128)S(1)}, f32[4,128,128]{2,1,0:T(8,128)S(1)}, u32[]{:S(2)}, u32[]{:S(2)}) %collective-permute-start) | collective-permute-done | bytes 262176 | tf_op jit(solution)/shard_map/while/body/eval_jaxpr/ppermute | solution.py:16
  573.7 9.8 %collective-permute-done = f32[4,128,128]{2,1,0:T(8,128)S(1)} collective-permute-done((f32[4,128,128]{2,1,0:T(8,128)S(1)}, f32[4,128,128]{2,1,0:T(8,128)S(1)}, u32[]{:S(2)}, u32[]{:S(2)}) %collective-permute-start) | collective-permute-done | bytes 262176 | tf_op jit(solution)/shard_map/while/body/eval_jaxpr/ppermute | solution.py:16
  585.8 8.4 %collective-permute-done = f32[4,128,128]{2,1,0:T(8,128)S(1)} collective-permute-done((f32[4,128,128]{2,1,0:T(8,128)S(1)}, f32[4,128,128]{2,1,0:T(8,128)S(1)}, u32[]{:S(2)}, u32[]{:S(2)}) %collective-permute-start) | collective-permute-done | bytes 262176 | tf_op jit(solution)/shard_map/while/body/eval_jaxpr/ppermute | solution.py:16
  596.6 8.4 %collective-permute-done = f32[4,128,128]{2,1,0:T(8,128)S(1)} collective-permute-done((f32[4,128,128]{2,1,0:T(8,128)S(1)}, f32[4,128,128]{2,1,0:T(8,128)S(1)}, u32[]{:S(2)}, u32[]{:S(2)}) %collective-permute-start) | collective-permute-done | bytes 262176 | tf_op jit(solution)/shard_map/while/body/eval_jaxpr/ppermute | solution.py:16
  615.9 21.4 %while.38 = (s32[]{:T(128)}, f32[4,128,128]{2,1,0:T(8,128)S(1)}, f32[8,4,64,128]{3,2,1,0:T(8,128)S(1)}, f32[8,4,128,128]{3,2,1,0:T(8,128)}, f32[8,4,64,128]{3,2,1,0:T(8,128)}, /*index=5*/s32[]{:T(128)}) while((s32[]{:T(128)}, f32[4,128,128]{2,1,0:T(8,128)S(1)}, f32[8,4,64,128]{3,2,1,0:T(8,128)S(1)}, f32[8,4,128,128]{3,2,1,0:T(8,128)}, ...), condition=%wide.region_8.9_spmd, body=%wide.region_7.8_spmd.sunk | while | flops 150994944 | bytes 1836113 | solution.py:154
  641.6 14.6 %all_to_all.19 = bf16[8,64,512]{2,1,0:T(8,128)(2,1)S(1)} all-to-all(bf16[8,64,512]{2,1,0:T(8,128)(2,1)S(1)} %bitcast.148), channel_id=1, replica_groups=mesh['ctx'=32,'head'=8] {'head'}, dimensions={0} | all-to-all | bytes 1048576 | tf_op jit(solution)/shard_map/all_to_all | solution.py:164
  (224 shorter events, 232.8 us)
Async XLA Ops:
  0.7 18.5 %collective-permute-start.1 = (bf16[3,256]{1,0:T(4,128)(2,1)S(1)}, bf16[3,256]{1,0:T(4,128)(2,1)S(1)}, u32[]{:S(2)}, u32[]{:S(2)}) collective-permute-start(bf16[3,256]{1,0:T(4,128)(2,1)S(1)} %slice.81), channel_id=1, source_target_pairs={{0,8},{8,16},{16,24},{24,32},{32,40},{40,48},{48,56},{56,64},{64,7... | collective-permute-start | bytes 4616 | tf_op jit(solution)/shard_map/ppermute | solution.py:16
  5.2 191.8 %collective-permute-start.2 = (bf16[3,512]{1,0:T(4,128)(2,1)S(1)}, bf16[3,512]{1,0:T(4,128)(2,1)S(1)}, u32[]{:S(2)}, u32[]{:S(2)}) collective-permute-start(bf16[3,512]{1,0:T(4,128)(2,1)S(1)} %slice.89), channel_id=1, source_target_pairs={{0,8},{8,16},{16,24},{24,32},{32,40},{40,48},{48,56},{56,64},{64,7... | collective-permute-start | bytes 9224 | tf_op jit(solution)/shard_map/ppermute | solution.py:16
  9.8 172.9 %collective-permute-start.3 = (bf16[3,256]{1,0:T(4,128)(2,1)S(1)}, bf16[3,256]{1,0:T(4,128)(2,1)S(1)}, u32[]{:S(2)}, u32[]{:S(2)}) collective-permute-start(bf16[3,256]{1,0:T(4,128)(2,1)S(1)} %slice.97), channel_id=1, source_target_pairs={{0,8},{8,16},{16,24},{24,32},{32,40},{40,48},{48,56},{56,64},{64,7... | collective-permute-start | bytes 4616 | tf_op jit(solution)/shard_map/ppermute | solution.py:16
  258.8 11.2 %collective-permute-start = (f32[4,128,128]{2,1,0:T(8,128)S(1)}, f32[4,128,128]{2,1,0:T(8,128)S(1)}, u32[]{:S(2)}, u32[]{:S(2)}) collective-permute-start(f32[4,128,128]{2,1,0:T(8,128)S(1)} %convolution_add_fusion.5), channel_id=1, source_target_pairs={{0,8},{8,16},{16,24},{24,32},{32,40},{40,48},{48,56},{56,64},{64,7... | collective-permute-start | bytes 786440 | tf_op jit(solution)/shard_map/while/body/eval_jaxpr/ppermute | solution.py:16
  270.4 10.4 %collective-permute-start = (f32[4,128,128]{2,1,0:T(8,128)S(1)}, f32[4,128,128]{2,1,0:T(8,128)S(1)}, u32[]{:S(2)}, u32[]{:S(2)}) collective-permute-start(f32[4,128,128]{2,1,0:T(8,128)S(1)} %convolution_add_fusion.5), channel_id=1, source_target_pairs={{0,8},{8,16},{16,24},{24,32},{32,40},{40,48},{48,56},{56,64},{64,7... | collective-permute-start | bytes 786440 | tf_op jit(solution)/shard_map/while/body/eval_jaxpr/ppermute | solution.py:16
  281.2 10.4 %collective-permute-start = (f32[4,128,128]{2,1,0:T(8,128)S(1)}, f32[4,128,128]{2,1,0:T(8,128)S(1)}, u32[]{:S(2)}, u32[]{:S(2)}) collective-permute-start(f32[4,128,128]{2,1,0:T(8,128)S(1)} %convolution_add_fusion.5), channel_id=1, source_target_pairs={{0,8},{8,16},{16,24},{24,32},{32,40},{40,48},{48,56},{56,64},{64,7... | collective-permute-start | bytes 786440 | tf_op jit(solution)/shard_map/while/body/eval_jaxpr/ppermute | solution.py:16
  292.0 10.4 %collective-permute-start = (f32[4,128,128]{2,1,0:T(8,128)S(1)}, f32[4,128,128]{2,1,0:T(8,128)S(1)}, u32[]{:S(2)}, u32[]{:S(2)}) collective-permute-start(f32[4,128,128]{2,1,0:T(8,128)S(1)} %convolution_add_fusion.5), channel_id=1, source_target_pairs={{0,8},{8,16},{16,24},{24,32},{32,40},{40,48},{48,56},{56,64},{64,7... | collective-permute-start | bytes 786440 | tf_op jit(solution)/shard_map/while/body/eval_jaxpr/ppermute | solution.py:16
  302.7 10.4 %collective-permute-start = (f32[4,128,128]{2,1,0:T(8,128)S(1)}, f32[4,128,128]{2,1,0:T(8,128)S(1)}, u32[]{:S(2)}, u32[]{:S(2)}) collective-permute-start(f32[4,128,128]{2,1,0:T(8,128)S(1)} %convolution_add_fusion.5), channel_id=1, source_target_pairs={{0,8},{8,16},{16,24},{24,32},{32,40},{40,48},{48,56},{56,64},{64,7... | collective-permute-start | bytes 786440 | tf_op jit(solution)/shard_map/while/body/eval_jaxpr/ppermute | solution.py:16
  313.5 11.0 %collective-permute-start = (f32[4,128,128]{2,1,0:T(8,128)S(1)}, f32[4,128,128]{2,1,0:T(8,128)S(1)}, u32[]{:S(2)}, u32[]{:S(2)}) collective-permute-start(f32[4,128,128]{2,1,0:T(8,128)S(1)} %convolution_add_fusion.5), channel_id=1, source_target_pairs={{0,8},{8,16},{16,24},{24,32},{32,40},{40,48},{48,56},{56,64},{64,7... | collective-permute-start | bytes 786440 | tf_op jit(solution)/shard_map/while/body/eval_jaxpr/ppermute | solution.py:16
  324.9 12.1 %collective-permute-start = (f32[4,128,128]{2,1,0:T(8,128)S(1)}, f32[4,128,128]{2,1,0:T(8,128)S(1)}, u32[]{:S(2)}, u32[]{:S(2)}) collective-permute-start(f32[4,128,128]{2,1,0:T(8,128)S(1)} %convolution_add_fusion.5), channel_id=1, source_target_pairs={{0,8},{8,16},{16,24},{24,32},{32,40},{40,48},{48,56},{56,64},{64,7... | collective-permute-start | bytes 786440 | tf_op jit(solution)/shard_map/while/body/eval_jaxpr/ppermute | solution.py:16
  337.4 13.1 %collective-permute-start = (f32[4,128,128]{2,1,0:T(8,128)S(1)}, f32[4,128,128]{2,1,0:T(8,128)S(1)}, u32[]{:S(2)}, u32[]{:S(2)}) collective-permute-start(f32[4,128,128]{2,1,0:T(8,128)S(1)} %convolution_add_fusion.5), channel_id=1, source_target_pairs={{0,8},{8,16},{16,24},{24,32},{32,40},{40,48},{48,56},{56,64},{64,7... | collective-permute-start | bytes 786440 | tf_op jit(solution)/shard_map/while/body/eval_jaxpr/ppermute | solution.py:16
  350.9 12.2 %collective-permute-start = (f32[4,128,128]{2,1,0:T(8,128)S(1)}, f32[4,128,128]{2,1,0:T(8,128)S(1)}, u32[]{:S(2)}, u32[]{:S(2)}) collective-permute-start(f32[4,128,128]{2,1,0:T(8,128)S(1)} %convolution_add_fusion.5), channel_id=1, source_target_pairs={{0,8},{8,16},{16,24},{24,32},{32,40},{40,48},{48,56},{56,64},{64,7... | collective-permute-start | bytes 786440 | tf_op jit(solution)/shard_map/while/body/eval_jaxpr/ppermute | solution.py:16
  363.6 11.4 %collective-permute-start = (f32[4,128,128]{2,1,0:T(8,128)S(1)}, f32[4,128,128]{2,1,0:T(8,128)S(1)}, u32[]{:S(2)}, u32[]{:S(2)}) collective-permute-start(f32[4,128,128]{2,1,0:T(8,128)S(1)} %convolution_add_fusion.5), channel_id=1, source_target_pairs={{0,8},{8,16},{16,24},{24,32},{32,40},{40,48},{48,56},{56,64},{64,7... | collective-permute-start | bytes 786440 | tf_op jit(solution)/shard_map/while/body/eval_jaxpr/ppermute | solution.py:16
  375.4 10.5 %collective-permute-start = (f32[4,128,128]{2,1,0:T(8,128)S(1)}, f32[4,128,128]{2,1,0:T(8,128)S(1)}, u32[]{:S(2)}, u32[]{:S(2)}) collective-permute-start(f32[4,128,128]{2,1,0:T(8,128)S(1)} %convolution_add_fusion.5), channel_id=1, source_target_pairs={{0,8},{8,16},{16,24},{24,32},{32,40},{40,48},{48,56},{56,64},{64,7... | collective-permute-start | bytes 786440 | tf_op jit(solution)/shard_map/while/body/eval_jaxpr/ppermute | solution.py:16
  386.3 10.4 %collective-permute-start = (f32[4,128,128]{2,1,0:T(8,128)S(1)}, f32[4,128,128]{2,1,0:T(8,128)S(1)}, u32[]{:S(2)}, u32[]{:S(2)}) collective-permute-start(f32[4,128,128]{2,1,0:T(8,128)S(1)} %convolution_add_fusion.5), channel_id=1, source_target_pairs={{0,8},{8,16},{16,24},{24,32},{32,40},{40,48},{48,56},{56,64},{64,7... | collective-permute-start | bytes 786440 | tf_op jit(solution)/shard_map/while/body/eval_jaxpr/ppermute | solution.py:16
  397.1 10.4 %collective-permute-start = (f32[4,128,128]{2,1,0:T(8,128)S(1)}, f32[4,128,128]{2,1,0:T(8,128)S(1)}, u32[]{:S(2)}, u32[]{:S(2)}) collective-permute-start(f32[4,128,128]{2,1,0:T(8,128)S(1)} %convolution_add_fusion.5), channel_id=1, source_target_pairs={{0,8},{8,16},{16,24},{24,32},{32,40},{40,48},{48,56},{56,64},{64,7... | collective-permute-start | bytes 786440 | tf_op jit(solution)/shard_map/while/body/eval_jaxpr/ppermute | solution.py:16
  407.8 10.4 %collective-permute-start = (f32[4,128,128]{2,1,0:T(8,128)S(1)}, f32[4,128,128]{2,1,0:T(8,128)S(1)}, u32[]{:S(2)}, u32[]{:S(2)}) collective-permute-start(f32[4,128,128]{2,1,0:T(8,128)S(1)} %convolution_add_fusion.5), channel_id=1, source_target_pairs={{0,8},{8,16},{16,24},{24,32},{32,40},{40,48},{48,56},{56,64},{64,7... | collective-permute-start | bytes 786440 | tf_op jit(solution)/shard_map/while/body/eval_jaxpr/ppermute | solution.py:16
  418.6 10.5 %collective-permute-start = (f32[4,128,128]{2,1,0:T(8,128)S(1)}, f32[4,128,128]{2,1,0:T(8,128)S(1)}, u32[]{:S(2)}, u32[]{:S(2)}) collective-permute-start(f32[4,128,128]{2,1,0:T(8,128)S(1)} %convolution_add_fusion.5), channel_id=1, source_target_pairs={{0,8},{8,16},{16,24},{24,32},{32,40},{40,48},{48,56},{56,64},{64,7... | collective-permute-start | bytes 786440 | tf_op jit(solution)/shard_map/while/body/eval_jaxpr/ppermute | solution.py:16
  429.5 11.7 %collective-permute-start = (f32[4,128,128]{2,1,0:T(8,128)S(1)}, f32[4,128,128]{2,1,0:T(8,128)S(1)}, u32[]{:S(2)}, u32[]{:S(2)}) collective-permute-start(f32[4,128,128]{2,1,0:T(8,128)S(1)} %convolution_add_fusion.5), channel_id=1, source_target_pairs={{0,8},{8,16},{16,24},{24,32},{32,40},{40,48},{48,56},{56,64},{64,7... | collective-permute-start | bytes 786440 | tf_op jit(solution)/shard_map/while/body/eval_jaxpr/ppermute | solution.py:16
  441.6 12.8 %collective-permute-start = (f32[4,128,128]{2,1,0:T(8,128)S(1)}, f32[4,128,128]{2,1,0:T(8,128)S(1)}, u32[]{:S(2)}, u32[]{:S(2)}) collective-permute-start(f32[4,128,128]{2,1,0:T(8,128)S(1)} %convolution_add_fusion.5), channel_id=1, source_target_pairs={{0,8},{8,16},{16,24},{24,32},{32,40},{40,48},{48,56},{56,64},{64,7... | collective-permute-start | bytes 786440 | tf_op jit(solution)/shard_map/while/body/eval_jaxpr/ppermute | solution.py:16
  454.8 12.4 %collective-permute-start = (f32[4,128,128]{2,1,0:T(8,128)S(1)}, f32[4,128,128]{2,1,0:T(8,128)S(1)}, u32[]{:S(2)}, u32[]{:S(2)}) collective-permute-start(f32[4,128,128]{2,1,0:T(8,128)S(1)} %convolution_add_fusion.5), channel_id=1, source_target_pairs={{0,8},{8,16},{16,24},{24,32},{32,40},{40,48},{48,56},{56,64},{64,7... | collective-permute-start | bytes 786440 | tf_op jit(solution)/shard_map/while/body/eval_jaxpr/ppermute | solution.py:16
  467.6 11.6 %collective-permute-start = (f32[4,128,128]{2,1,0:T(8,128)S(1)}, f32[4,128,128]{2,1,0:T(8,128)S(1)}, u32[]{:S(2)}, u32[]{:S(2)}) collective-permute-start(f32[4,128,128]{2,1,0:T(8,128)S(1)} %convolution_add_fusion.5), channel_id=1, source_target_pairs={{0,8},{8,16},{16,24},{24,32},{32,40},{40,48},{48,56},{56,64},{64,7... | collective-permute-start | bytes 786440 | tf_op jit(solution)/shard_map/while/body/eval_jaxpr/ppermute | solution.py:16
  479.6 10.7 %collective-permute-start = (f32[4,128,128]{2,1,0:T(8,128)S(1)}, f32[4,128,128]{2,1,0:T(8,128)S(1)}, u32[]{:S(2)}, u32[]{:S(2)}) collective-permute-start(f32[4,128,128]{2,1,0:T(8,128)S(1)} %convolution_add_fusion.5), channel_id=1, source_target_pairs={{0,8},{8,16},{16,24},{24,32},{32,40},{40,48},{48,56},{56,64},{64,7... | collective-permute-start | bytes 786440 | tf_op jit(solution)/shard_map/while/body/eval_jaxpr/ppermute | solution.py:16
  490.7 10.4 %collective-permute-start = (f32[4,128,128]{2,1,0:T(8,128)S(1)}, f32[4,128,128]{2,1,0:T(8,128)S(1)}, u32[]{:S(2)}, u32[]{:S(2)}) collective-permute-start(f32[4,128,128]{2,1,0:T(8,128)S(1)} %convolution_add_fusion.5), channel_id=1, source_target_pairs={{0,8},{8,16},{16,24},{24,32},{32,40},{40,48},{48,56},{56,64},{64,7... | collective-permute-start | bytes 786440 | tf_op jit(solution)/shard_map/while/body/eval_jaxpr/ppermute | solution.py:16
  501.5 10.4 %collective-permute-start = (f32[4,128,128]{2,1,0:T(8,128)S(1)}, f32[4,128,128]{2,1,0:T(8,128)S(1)}, u32[]{:S(2)}, u32[]{:S(2)}) collective-permute-start(f32[4,128,128]{2,1,0:T(8,128)S(1)} %convolution_add_fusion.5), channel_id=1, source_target_pairs={{0,8},{8,16},{16,24},{24,32},{32,40},{40,48},{48,56},{56,64},{64,7... | collective-permute-start | bytes 786440 | tf_op jit(solution)/shard_map/while/body/eval_jaxpr/ppermute | solution.py:16
  512.3 10.4 %collective-permute-start = (f32[4,128,128]{2,1,0:T(8,128)S(1)}, f32[4,128,128]{2,1,0:T(8,128)S(1)}, u32[]{:S(2)}, u32[]{:S(2)}) collective-permute-start(f32[4,128,128]{2,1,0:T(8,128)S(1)} %convolution_add_fusion.5), channel_id=1, source_target_pairs={{0,8},{8,16},{16,24},{24,32},{32,40},{40,48},{48,56},{56,64},{64,7... | collective-permute-start | bytes 786440 | tf_op jit(solution)/shard_map/while/body/eval_jaxpr/ppermute | solution.py:16
  523.0 10.4 %collective-permute-start = (f32[4,128,128]{2,1,0:T(8,128)S(1)}, f32[4,128,128]{2,1,0:T(8,128)S(1)}, u32[]{:S(2)}, u32[]{:S(2)}) collective-permute-start(f32[4,128,128]{2,1,0:T(8,128)S(1)} %convolution_add_fusion.5), channel_id=1, source_target_pairs={{0,8},{8,16},{16,24},{24,32},{32,40},{40,48},{48,56},{56,64},{64,7... | collective-permute-start | bytes 786440 | tf_op jit(solution)/shard_map/while/body/eval_jaxpr/ppermute | solution.py:16
  533.8 11.5 %collective-permute-start = (f32[4,128,128]{2,1,0:T(8,128)S(1)}, f32[4,128,128]{2,1,0:T(8,128)S(1)}, u32[]{:S(2)}, u32[]{:S(2)}) collective-permute-start(f32[4,128,128]{2,1,0:T(8,128)S(1)} %convolution_add_fusion.5), channel_id=1, source_target_pairs={{0,8},{8,16},{16,24},{24,32},{32,40},{40,48},{48,56},{56,64},{64,7... | collective-permute-start | bytes 786440 | tf_op jit(solution)/shard_map/while/body/eval_jaxpr/ppermute | solution.py:16
  545.7 12.6 %collective-permute-start = (f32[4,128,128]{2,1,0:T(8,128)S(1)}, f32[4,128,128]{2,1,0:T(8,128)S(1)}, u32[]{:S(2)}, u32[]{:S(2)}) collective-permute-start(f32[4,128,128]{2,1,0:T(8,128)S(1)} %convolution_add_fusion.5), channel_id=1, source_target_pairs={{0,8},{8,16},{16,24},{24,32},{32,40},{40,48},{48,56},{56,64},{64,7... | collective-permute-start | bytes 786440 | tf_op jit(solution)/shard_map/while/body/eval_jaxpr/ppermute | solution.py:16
  558.8 12.6 %collective-permute-start = (f32[4,128,128]{2,1,0:T(8,128)S(1)}, f32[4,128,128]{2,1,0:T(8,128)S(1)}, u32[]{:S(2)}, u32[]{:S(2)}) collective-permute-start(f32[4,128,128]{2,1,0:T(8,128)S(1)} %convolution_add_fusion.5), channel_id=1, source_target_pairs={{0,8},{8,16},{16,24},{24,32},{32,40},{40,48},{48,56},{56,64},{64,7... | collective-permute-start | bytes 786440 | tf_op jit(solution)/shard_map/while/body/eval_jaxpr/ppermute | solution.py:16
  571.8 11.7 %collective-permute-start = (f32[4,128,128]{2,1,0:T(8,128)S(1)}, f32[4,128,128]{2,1,0:T(8,128)S(1)}, u32[]{:S(2)}, u32[]{:S(2)}) collective-permute-start(f32[4,128,128]{2,1,0:T(8,128)S(1)} %convolution_add_fusion.5), channel_id=1, source_target_pairs={{0,8},{8,16},{16,24},{24,32},{32,40},{40,48},{48,56},{56,64},{64,7... | collective-permute-start | bytes 786440 | tf_op jit(solution)/shard_map/while/body/eval_jaxpr/ppermute | solution.py:16
  594.7 10.4 %collective-permute-start = (f32[4,128,128]{2,1,0:T(8,128)S(1)}, f32[4,128,128]{2,1,0:T(8,128)S(1)}, u32[]{:S(2)}, u32[]{:S(2)}) collective-permute-start(f32[4,128,128]{2,1,0:T(8,128)S(1)} %convolution_add_fusion.5), channel_id=1, source_target_pairs={{0,8},{8,16},{16,24},{24,32},{32,40},{40,48},{48,56},{56,64},{64,7... | collective-permute-start | bytes 786440 | tf_op jit(solution)/shard_map/while/body/eval_jaxpr/ppermute | solution.py:16
  (7 other events, 205.7 us)
where the time goes:
time: 660 us; the launch traced here: 657 us
  waiting for transfers between devices  281 us (43%)
  other arithmetic  169 us (26%)
  matrix products  101 us (15%)
  starting transfers between devices  75.1 us (11%)
  blocking collectives  14.6 us (2%)
  local copies, waits for them, and re-layouts  14.4 us (2%)
    ppermute x34, waiting for transfers between devices, shifted(): lax.ppermute(value, axis, [(source, source + steps) for source in range(f...  281 us
    another operation x3, other arithmetic, group_terms(): lax.linalg.triangular_solve(identity_mats + strict, identity_mats, left_s...  157 us
    ppermute x34, starting transfers between devices, shifted(): lax.ppermute(value, axis, [(source, source + steps) for source in range(f...  75.1 us
    dot_general x56, matrix products, matmul_pair(): jnp.einsum('...ij,...jk->...ik', left_mats, right_mats, precision=highest)  46.4 us
    all_to_all x1, blocking collectives, body(): lax.all_to_all(normed, 'head', split_axis=0, concat_axis=1, tiled=True)  14.6 us
  transfers between devices with their start and end apart: 34, of which 31 were waited for; matrix products, arithmetic and copies ran while one was open for 28% of the time, Pallas kernels for 0%

commit v1 on v0

--- a/solution.py
+++ b/solution.py
@@ -25,6 +25,23 @@
 
 def unit_rows(matrix):
     return matrix * lax.rsqrt(jnp.sum(matrix * matrix, axis=-1, keepdims=True) + norm_eps)
+
+
+def unit_lower_inverse(strict, row_ids, col_ids):
+    length = strict.shape[-1]
+    eye = (row_ids == col_ids).astype(jnp.float32)
+    inverse = eye - jnp.where(row_ids // 2 == col_ids // 2, strict, 0.0)
+
+    def level(depth, inverse):
+        width = 2 << depth
+        lower_left = jnp.where(
+            (row_ids // (2 * width) == col_ids // (2 * width)) & (row_ids // width != col_ids // width),
+            strict,
+            0.0,
+        )
+        return inverse - matmul_pair(matmul_pair(inverse, lower_left), inverse)
+
+    return lax.fori_loop(0, length.bit_length() - 2, level, inverse)
 
 
 def group_terms(query, keys, values, beta, logdecay):
@@ -37,10 +54,7 @@
     decay_mask = jnp.where(inside, jnp.exp(jnp.where(inside, differ, 0.0)), 0.0)
     keygram = jnp.einsum("...ik,...jk->...ij", keys, keys, precision=highest)
     strict = jnp.where(col_ids < row_ids, beta[..., :, None] * keygram * decay_mask, 0.0)
-    identity_mats = jnp.broadcast_to(jnp.eye(length, dtype=jnp.float32), strict.shape)
-    inverse = lax.linalg.triangular_solve(
-        identity_mats + strict, identity_mats, left_side=True, lower=True, unit_diagonal=True
-    )
+    inverse = unit_lower_inverse(strict, row_ids, col_ids)
     upd_values = jnp.einsum(
         "...ij,...jd->...id", inverse, beta[..., None] * values, precision=highest
     )
@@ -142,10 +156,19 @@
         local_step, (zero_state, identity_state), (terms, group_maps)
     )
 
-    def chain_turn(turn, incoming_state):
-        return shifted(matmul_pair(shard_map_mat, incoming_state) + local_state, "ctx", 1)
-
-    incoming = lax.fori_loop(0, lax.axis_size("ctx") - 1, chain_turn, zero_state)
+    ctx_count = lax.axis_size("ctx")
+    span_map, span_state = shard_map_mat, local_state
+    reach = 1
+    while reach < ctx_count:
+        if 2 * reach < ctx_count:
+            prior_map, prior_state = shifted((span_map, span_state), "ctx", reach)
+            span_state = matmul_pair(span_map, prior_state) + span_state
+            span_map = matmul_pair(span_map, prior_map)
+        else:
+            prior_state = shifted(span_state, "ctx", reach)
+            span_state = matmul_pair(span_map, prior_state) + span_state
+        reach *= 2
+    incoming = shifted(span_state, "ctx", 1)
 
     def carried_step(state, packed):
         effect_group, group_map = packed

time: 660 us -> 275 us (0.42)
  waiting for transfers between devices: 281 us -> 28.2 us
  other arithmetic: 169 us -> 19.1 us
  matrix products: 101 us -> 112 us
  local copies, waits for them, and re-layouts: 14.4 us -> 23.9 us
    ppermute x34 -> x13, waiting for transfers between devices: 281 us -> 28.2 us  [shifted(): lax.ppermute(value, axis, [(source, source + steps) for source in range(f...]
    another operation x3 -> x0, other arithmetic: 157 us -> none  [group_terms(): lax.linalg.triangular_solve(identity_mats + strict, identity_mats, left_s...]
    dot_general x56 -> x44, matrix products: 46.4 us -> 53 us  [matmul_pair(): jnp.einsum('...ij,...jk->...ik', left_mats, right_mats, precision=highest)]
    ppermute x34 -> x13, starting transfers between devices: 75.1 us -> 73.3 us  [shifted(): lax.ppermute(value, axis, [(source, source + steps) for source in range(f...]
  transfers between devices with their start and end apart: 34 -> 13, of which waited for: 31 -> 10; matrix products, arithmetic and copies ran while one was open for 28% -> 21% of each run, Pallas kernels for 0% -> 0%
where the time goes in v1:
time: 275 us; the launch traced here: 272 us
  matrix products  112 us (41%)
  starting transfers between devices  73.3 us (27%)
  waiting for transfers between devices  28.2 us (10%)
  local copies, waits for them, and re-layouts  23.9 us (9%)
  other arithmetic  19.1 us (7%)
  blocking collectives  14.2 us (5%)
    ppermute x13, starting transfers between devices, shifted(): lax.ppermute(value, axis, [(source, source + steps) for source in range(f...  73.3 us
    dot_general x44, matrix products, matmul_pair(): jnp.einsum('...ij,...jk->...ik', left_mats, right_mats, precision=highest)  53 us
    ppermute x13, waiting for transfers between devices, shifted(): lax.ppermute(value, axis, [(source, source + steps) for source in range(f...  28.2 us
    dot_general x8, matrix products, group_step(): jnp.einsum('...ik,...kd->...id', query_decay, state, precision=highest)  15.4 us
    all_to_all x1, blocking collectives, body(): lax.all_to_all(normed, 'head', split_axis=0, concat_axis=1, tiled=True)  14.2 us
    dot_general x8, matrix products, group_step(): jnp.einsum('...ik,...id->...kd', key_decay, new_values, precision=highest)  12.1 us
    dot_general x8, matrix products, group_step(): jnp.einsum('...ik,...kd->...id', upd_keys, state, precision=highest)  10.1 us
    dot_general x8, matrix products, group_step(): jnp.einsum('...ij,...jd->...id', scores, new_values, precision=highest)  9.32 us
  transfers between devices with their start and end apart: 13, of which 10 were waited for; matrix products, arithmetic and copies ran while one was open for 21% of the time, Pallas kernels for 0%

profile of v1, /device:TPU:4, one launch (start us, length us, event | category | flops | bytes accessed | tf_op | source)
XLA Modules:
  0.0 271.9 jit_solution(7220894989862106338)
XLA Ops:
  0.7 3.8 %collective-permute-start = (bf16[3,256]{1,0:T(4,128)(2,1)S(1)}, bf16[3,256]{1,0:T(4,128)(2,1)S(1)}, u32[]{:S(2)}, u32[]{:S(2)}) collective-permute-start(bf16[3,256]{1,0:T(4,128)(2,1)S(1)} %slice.77), channel_id=1, source_target_pairs={{0,8},{8,16},{16,24},{24,32},{32,40},{40,48},{48,56},{56,64},{64,7... | collective-permute-start | bytes 4616 | tf_op jit(solution)/shard_map/ppermute | solution.py:16
  5.8 3.8 %collective-permute-start.1 = (bf16[3,512]{1,0:T(4,128)(2,1)}, bf16[3,512]{1,0:T(4,128)(2,1)}, u32[]{:S(2)}, u32[]{:S(2)}) collective-permute-start(bf16[3,512]{1,0:T(4,128)(2,1)} %slice.85), channel_id=1, source_target_pairs={{0,8},{8,16},{16,24},{24,32},{32,40},{40,48},{48,56},{56,64},{64,7... | collective-permute-start | bytes 9224 | tf_op jit(solution)/shard_map/ppermute | solution.py:16
  10.9 3.8 %collective-permute-start.2 = (bf16[3,256]{1,0:T(4,128)(2,1)}, bf16[3,256]{1,0:T(4,128)(2,1)}, u32[]{:S(2)}, u32[]{:S(2)}) collective-permute-start(bf16[3,256]{1,0:T(4,128)(2,1)} %slice.93), channel_id=1, source_target_pairs={{0,8},{8,16},{16,24},{24,32},{32,40},{40,48},{48,56},{56,64},{64,7... | collective-permute-start | bytes 4616 | tf_op jit(solution)/shard_map/ppermute | solution.py:16
  29.2 19.8 %while.46 = (s32[]{:T(128)}, f32[8,4,64,64]{3,2,1,0:T(8,128)S(1)}, f32[8,4,64,64]{2,3,1,0:T(8,128)S(1)}, s32[]{:T(128)}, s32[]{:T(128)}) while((s32[]{:T(128)}, f32[8,4,64,64]{3,2,1,0:T(8,128)S(1)}, f32[8,4,64,64]{2,3,1,0:T(8,128)S(1)}, s32[]{:T(128)}, s32[]{:T(128)}) %tuple.99), condition=%wide.region_3.4_spmd.clone.clone, body=%wide.region_2.3_spmd.clone.clone.sunk | while | flops 201723904 | bytes 4202621 | solution.py:44
  56.1 5.1 %multiply_subtract_fusion = f32[8,4,128,128]{3,2,1,0:T(8,128)} fusion(f32[8,4,64,128]{3,2,1,0:T(8,128)S(1)} %fusion.73, f32[128,128]{1,0:T(8,128)S(1)} %fusion.89, f32[8,4]{1,0:T(8,128)S(1)} %copy.96, f32[8,4,64,128]{3,2,0,1:T(8,128)S(1)} %get-tuple-element.469), kind=kOutput, calls=%fused_computation.81 | convolution fusion | flops 403701760 | bytes 4259968 | tf_op jit(solution)/shard_map/...ik,...ij->...kj/dot_general | solution.py:143
  63.6 2.4 fusion.81
  66.1 2.5 reshape.113
  68.6 3.4 %fusion.72 = f32[8,4,64,128]{3,2,1,0:T(8,128)} fusion(f32[8,4,64,64]{3,2,1,0:T(8,128)S(1)} %get-tuple-element.281, f32[8,64,4,128]{3,2,1,0:T(4,128)} %reshape.113, f32[8,4,64]{2,1,0:T(4,128)S(1)} %copy.87), kind=kOutput, calls=%fused_computation.103 | convolution fusion | flops 201588736 | bytes 2629632 | tf_op jit(solution)/shard_map/...ij,...jd->...id/dot_general | solution.py:58
  73.1 63.8 %while.47 = (s32[]{:T(128)}, f32[4,128,128]{2,1,0:T(8,128)S(1)}, f32[4,128,128]{2,1,0:T(8,128)S(1)}, f32[8,4,64,128]{3,2,1,0:T(8,128)}, f32[8,4]{1,0:T(8,128)}, ...) while((s32[]{:T(128)}, f32[4,128,128]{2,1,0:T(8,128)S(1)}, ...), condition=%wide.region_6.7_spmd.clone, body=%wide.region_5.6_spmd.clone.sunk | while | flops 277217280 | bytes 3804367 | solution.py:155
  75.5 1.9 fusion.184
  83.5 1.9 fusion.184
  107.4 1.9 fusion.184
  115.4 1.9 fusion.184
  123.4 1.9 fusion.184
  131.4 1.9 fusion.184
  136.9 5.0 %collective-permute-start.7 = (f32[4,128,128]{2,1,0:T(8,128)S(1)}, f32[4,128,128]{2,1,0:T(8,128)S(1)}, u32[]{:S(2)}, u32[]{:S(2)}) collective-permute-start(f32[4,128,128]{2,1,0:T(8,128)S(1)} %get-tuple-element.284), channel_id=1, source_target_pairs={{0,8},{8,16},{16,24},{24,32},{32,40},{40,48},{48,56},{56,64},{64,7... | collective-permute-start | bytes 786440 | tf_op jit(solution)/shard_map/ppermute | solution.py:16
  141.9 2.9 %collective-permute-start.3 = (f32[4,128,128]{2,1,0:T(8,128)S(1)}, f32[4,128,128]{2,1,0:T(8,128)S(1)}, u32[]{:S(2)}, u32[]{:S(2)}) collective-permute-start(f32[4,128,128]{2,1,0:T(8,128)S(1)} %get-tuple-element.283), channel_id=1, source_target_pairs={{0,8},{8,16},{16,24},{24,32},{32,40},{40,48},{48,56},{56,64},{64,7... | collective-permute-start | bytes 786440 | tf_op jit(solution)/shard_map/ppermute | solution.py:16
  144.9 4.1 %collective-permute-done.7 = f32[4,128,128]{2,1,0:T(8,128)S(1)} collective-permute-done((f32[4,128,128]{2,1,0:T(8,128)S(1)}, f32[4,128,128]{2,1,0:T(8,128)S(1)}, u32[]{:S(2)}, u32[]{:S(2)}) %collective-permute-start.7) | collective-permute-done | bytes 262176 | tf_op jit(solution)/shard_map/ppermute | solution.py:16
  149.4 4.5 %collective-permute-start.8 = (f32[4,128,128]{2,1,0:T(8,128)S(1)}, f32[4,128,128]{2,1,0:T(8,128)S(1)}, u32[]{:S(2)}, u32[]{:S(2)}) collective-permute-start(f32[4,128,128]{2,1,0:T(8,128)S(1)} %convolution_add_fusion.6), channel_id=1, source_target_pairs={{0,16},{8,24},{16,32},{24,40},{32,48},{40,56},{48,64},{56,72},{64,... | collective-permute-start | bytes 786440 | tf_op jit(solution)/shard_map/ppermute | solution.py:16
  155.9 5.6 %collective-permute-start.4 = (f32[4,128,128]{2,1,0:T(8,128)S(1)}, f32[4,128,128]{2,1,0:T(8,128)S(1)}, u32[]{:S(2)}, u32[]{:S(2)}) collective-permute-start(f32[4,128,128]{2,1,0:T(8,128)S(1)} %fusion.98), channel_id=1, source_target_pairs={{0,16},{8,24},{16,32},{24,40},{32,48},{40,56},{48,64},{56,72},{64,... | collective-permute-start | bytes 786440 | tf_op jit(solution)/shard_map/ppermute | solution.py:16
  161.6 3.8 %collective-permute-done.8 = f32[4,128,128]{2,1,0:T(8,128)S(1)} collective-permute-done((f32[4,128,128]{2,1,0:T(8,128)S(1)}, f32[4,128,128]{2,1,0:T(8,128)S(1)}, u32[]{:S(2)}, u32[]{:S(2)}) %collective-permute-start.8) | collective-permute-done | bytes 262176 | tf_op jit(solution)/shard_map/ppermute | solution.py:16
  165.7 6.8 %collective-permute-start.9 = (f32[4,128,128]{2,1,0:T(8,128)S(1)}, f32[4,128,128]{2,1,0:T(8,128)S(1)}, u32[]{:S(2)}, u32[]{:S(2)}) collective-permute-start(f32[4,128,128]{2,1,0:T(8,128)S(1)} %convolution_add_fusion.5), channel_id=1, source_target_pairs={{0,32},{8,40},{16,48},{24,56},{32,64},{40,72},{48,80},{56,88},{64,... | collective-permute-start | bytes 786440 | tf_op jit(solution)/shard_map/ppermute | solution.py:16
  172.6 6.1 %collective-permute-done.4 = f32[4,128,128]{2,1,0:T(8,128)S(1)} collective-permute-done((f32[4,128,128]{2,1,0:T(8,128)S(1)}, f32[4,128,128]{2,1,0:T(8,128)S(1)}, u32[]{:S(2)}, u32[]{:S(2)}) %collective-permute-start.4) | collective-permute-done | bytes 262176 | tf_op jit(solution)/shard_map/ppermute | solution.py:16
  179.0 6.9 %collective-permute-start.5 = (f32[4,128,128]{2,1,0:T(8,128)S(1)}, f32[4,128,128]{2,1,0:T(8,128)S(1)}, u32[]{:S(2)}, u32[]{:S(2)}) collective-permute-start(f32[4,128,128]{2,1,0:T(8,128)S(1)} %fusion.99), channel_id=1, source_target_pairs={{0,32},{8,40},{16,48},{24,56},{32,64},{40,72},{48,80},{56,88},{64,... | collective-permute-start | bytes 786440 | tf_op jit(solution)/shard_map/ppermute | solution.py:16
  186.8 11.4 %collective-permute-start.10 = (f32[4,128,128]{2,1,0:T(8,128)S(1)}, f32[4,128,128]{2,1,0:T(8,128)S(1)}, u32[]{:S(2)}, u32[]{:S(2)}) collective-permute-start(f32[4,128,128]{2,1,0:T(8,128)S(1)} %convolution_add_fusion.4), channel_id=1, source_target_pairs={{0,64},{8,72},{16,80},{24,88},{32,96},{40,104},{48,112},{56,120},{... | collective-permute-start | bytes 786440 | tf_op jit(solution)/shard_map/ppermute | solution.py:16
  199.8 2.1 collective-permute-start.6
  203.8 4.5 %collective-permute-done.6 = f32[4,128,128]{2,1,0:T(8,128)S(1)} collective-permute-done((f32[4,128,128]{2,1,0:T(8,128)S(1)}, f32[4,128,128]{2,1,0:T(8,128)S(1)}, u32[]{:S(2)}, u32[]{:S(2)}) %collective-permute-start.6) | collective-permute-done | bytes 262176 | tf_op jit(solution)/shard_map/ppermute | solution.py:16
  208.7 4.7 %collective-permute-done.11 = f32[4,128,128]{2,1,0:T(8,128)S(1)} collective-permute-done((f32[4,128,128]{2,1,0:T(8,128)S(1)}, f32[4,128,128]{2,1,0:T(8,128)S(1)}, u32[]{:S(2)}, u32[]{:S(2)}) %collective-permute-start.11) | collective-permute-done | bytes 262176 | tf_op jit(solution)/shard_map/ppermute | solution.py:16
  213.8 15.3 %collective-permute-start.12 = (f32[4,128,128]{2,1,0:T(8,128)S(1)}, f32[4,128,128]{2,1,0:T(8,128)S(1)}, u32[]{:S(2)}, u32[]{:S(2)}) collective-permute-start(f32[4,128,128]{2,1,0:T(8,128)S(1)} %convolution_add_fusion.2), channel_id=1, source_target_pairs={{0,8},{8,16},{16,24},{24,32},{32,40},{40,48},{48,56},{56,64},{64,7... | collective-permute-start | bytes 786440 | tf_op jit(solution)/shard_map/ppermute | solution.py:16
  229.1 2.3 convolution_subtract_fusion.2
  233.1 21.5 %while.45 = (s32[]{:T(128)}, f32[4,128,128]{2,1,0:T(8,128)S(1)}, f32[8,4,64,128]{3,2,1,0:T(8,128)S(1)}, f32[8,4,128,128]{3,2,1,0:T(8,128)}, f32[8,4,64,128]{3,2,1,0:T(8,128)}, /*index=5*/s32[]{:T(128)}) while((s32[]{:T(128)}, f32[4,128,128]{2,1,0:T(8,128)S(1)}, f32[8,4,64,128]{3,2,1,0:T(8,128)S(1)}, f32[8,4,128,128]{3,2,1,0:T(8,128)}, ...), condition=%wide.region_8.9_spmd, body=%wide.region_7.8_spmd.sunk | while | flops 150994944 | bytes 1836113 | solution.py:177
  256.8 14.2 %all_to_all.19 = bf16[8,64,512]{2,1,0:T(8,128)(2,1)S(1)} all-to-all(bf16[8,64,512]{2,1,0:T(8,128)(2,1)S(1)} %bitcast.164), channel_id=1, replica_groups=mesh['ctx'=32,'head'=8] {'head'}, dimensions={0} | all-to-all | bytes 1048576 | tf_op jit(solution)/shard_map/all_to_all | solution.py:187
  (201 shorter events, 133.7 us)
Async XLA Ops:
  0.0 203.8 %copy-start = (f32[128]{0:T(128)S(1)}, f32[128]{0:T(128)}, u32[]{:S(2)}) copy-start(f32[128]{0:T(128)} %param.25) | copy-start | bytes 1540
  0.7 23.7 %collective-permute-start = (bf16[3,256]{1,0:T(4,128)(2,1)S(1)}, bf16[3,256]{1,0:T(4,128)(2,1)S(1)}, u32[]{:S(2)}, u32[]{:S(2)}) collective-permute-start(bf16[3,256]{1,0:T(4,128)(2,1)S(1)} %slice.77), channel_id=1, source_target_pairs={{0,8},{8,16},{16,24},{24,32},{32,40},{40,48},{48,56},{56,64},{64,7... | collective-permute-start | bytes 4616 | tf_op jit(solution)/shard_map/ppermute | solution.py:16
  5.8 57.8 %collective-permute-start.1 = (bf16[3,512]{1,0:T(4,128)(2,1)}, bf16[3,512]{1,0:T(4,128)(2,1)}, u32[]{:S(2)}, u32[]{:S(2)}) collective-permute-start(bf16[3,512]{1,0:T(4,128)(2,1)} %slice.85), channel_id=1, source_target_pairs={{0,8},{8,16},{16,24},{24,32},{32,40},{40,48},{48,56},{56,64},{64,7... | collective-permute-start | bytes 9224 | tf_op jit(solution)/shard_map/ppermute | solution.py:16
  10.9 38.1 %collective-permute-start.2 = (bf16[3,256]{1,0:T(4,128)(2,1)}, bf16[3,256]{1,0:T(4,128)(2,1)}, u32[]{:S(2)}, u32[]{:S(2)}) collective-permute-start(bf16[3,256]{1,0:T(4,128)(2,1)} %slice.93), channel_id=1, source_target_pairs={{0,8},{8,16},{16,24},{24,32},{32,40},{40,48},{48,56},{56,64},{64,7... | collective-permute-start | bytes 4616 | tf_op jit(solution)/shard_map/ppermute | solution.py:16
  26.5 1.6 copy-start.7
  26.5 1.6 copy-start.8
  26.5 1.6 copy-start.12
  26.5 1.6 copy-start.13
  26.5 1.6 copy-start.15
  28.0 0.8 copy-start.3
  51.2 1.7 copy-start.4
  51.2 1.7 copy-start.9
  51.2 1.7 copy-start.14
  61.2 2.4 copy-start.5
  61.2 2.4 copy-start.10
  61.2 2.4 copy-start.11
  136.9 12.1 %collective-permute-start.7 = (f32[4,128,128]{2,1,0:T(8,128)S(1)}, f32[4,128,128]{2,1,0:T(8,128)S(1)}, u32[]{:S(2)}, u32[]{:S(2)}) collective-permute-start(f32[4,128,128]{2,1,0:T(8,128)S(1)} %get-tuple-element.284), channel_id=1, source_target_pairs={{0,8},{8,16},{16,24},{24,32},{32,40},{40,48},{48,56},{56,64},{64,7... | collective-permute-start | bytes 786440 | tf_op jit(solution)/shard_map/ppermute | solution.py:16
  141.9 13.6 %collective-permute-start.3 = (f32[4,128,128]{2,1,0:T(8,128)S(1)}, f32[4,128,128]{2,1,0:T(8,128)S(1)}, u32[]{:S(2)}, u32[]{:S(2)}) collective-permute-start(f32[4,128,128]{2,1,0:T(8,128)S(1)} %get-tuple-element.283), channel_id=1, source_target_pairs={{0,8},{8,16},{16,24},{24,32},{32,40},{40,48},{48,56},{56,64},{64,7... | collective-permute-start | bytes 786440 | tf_op jit(solution)/shard_map/ppermute | solution.py:16
  149.4 16.0 %collective-permute-start.8 = (f32[4,128,128]{2,1,0:T(8,128)S(1)}, f32[4,128,128]{2,1,0:T(8,128)S(1)}, u32[]{:S(2)}, u32[]{:S(2)}) collective-permute-start(f32[4,128,128]{2,1,0:T(8,128)S(1)} %convolution_add_fusion.6), channel_id=1, source_target_pairs={{0,16},{8,24},{16,32},{24,40},{32,48},{40,56},{48,64},{56,72},{64,... | collective-permute-start | bytes 786440 | tf_op jit(solution)/shard_map/ppermute | solution.py:16
  155.9 22.7 %collective-permute-start.4 = (f32[4,128,128]{2,1,0:T(8,128)S(1)}, f32[4,128,128]{2,1,0:T(8,128)S(1)}, u32[]{:S(2)}, u32[]{:S(2)}) collective-permute-start(f32[4,128,128]{2,1,0:T(8,128)S(1)} %fusion.98), channel_id=1, source_target_pairs={{0,16},{8,24},{16,32},{24,40},{32,48},{40,56},{48,64},{56,72},{64,... | collective-permute-start | bytes 786440 | tf_op jit(solution)/shard_map/ppermute | solution.py:16
  165.7 20.6 %collective-permute-start.9 = (f32[4,128,128]{2,1,0:T(8,128)S(1)}, f32[4,128,128]{2,1,0:T(8,128)S(1)}, u32[]{:S(2)}, u32[]{:S(2)}) collective-permute-start(f32[4,128,128]{2,1,0:T(8,128)S(1)} %convolution_add_fusion.5), channel_id=1, source_target_pairs={{0,32},{8,40},{16,48},{24,56},{32,64},{40,72},{48,80},{56,88},{64,... | collective-permute-start | bytes 786440 | tf_op jit(solution)/shard_map/ppermute | solution.py:16
  179.0 20.4 %collective-permute-start.5 = (f32[4,128,128]{2,1,0:T(8,128)S(1)}, f32[4,128,128]{2,1,0:T(8,128)S(1)}, u32[]{:S(2)}, u32[]{:S(2)}) collective-permute-start(f32[4,128,128]{2,1,0:T(8,128)S(1)} %fusion.99), channel_id=1, source_target_pairs={{0,32},{8,40},{16,48},{24,56},{32,64},{40,72},{48,80},{56,88},{64,... | collective-permute-start | bytes 786440 | tf_op jit(solution)/shard_map/ppermute | solution.py:16
  186.8 42.3 %copy-start.2 = (f32[8,4,64,64]{3,2,1,0:T(8,128)S(1)}, f32[8,4,64,64]{3,2,1,0:T(8,128)}, u32[]{:S(2)}) copy-start(f32[8,4,64,64]{3,2,1,0:T(8,128)} %get-tuple-element.685) | copy-start | bytes 1572868
  186.8 15.3 %collective-permute-start.10 = (f32[4,128,128]{2,1,0:T(8,128)S(1)}, f32[4,128,128]{2,1,0:T(8,128)S(1)}, u32[]{:S(2)}, u32[]{:S(2)}) collective-permute-start(f32[4,128,128]{2,1,0:T(8,128)S(1)} %convolution_add_fusion.4), channel_id=1, source_target_pairs={{0,64},{8,72},{16,80},{24,88},{32,96},{40,104},{48,112},{56,120},{... | collective-permute-start | bytes 786440 | tf_op jit(solution)/shard_map/ppermute | solution.py:16
  199.8 8.4 %collective-permute-start.6 = (f32[4,128,128]{2,1,0:T(8,128)S(1)}, f32[4,128,128]{2,1,0:T(8,128)S(1)}, u32[]{:S(2)}, u32[]{:S(2)}) collective-permute-start(f32[4,128,128]{2,1,0:T(8,128)S(1)} %fusion.100), channel_id=1, source_target_pairs={{0,64},{8,72},{16,80},{24,88},{32,96},{40,104},{48,112},{56,120},{... | collective-permute-start | bytes 786440 | tf_op jit(solution)/shard_map/ppermute | solution.py:16
  202.4 10.9 %collective-permute-start.11 = (f32[4,128,128]{2,1,0:T(8,128)S(1)}, f32[4,128,128]{2,1,0:T(8,128)S(1)}, u32[]{:S(2)}, u32[]{:S(2)}) collective-permute-start(f32[4,128,128]{2,1,0:T(8,128)S(1)} %convolution_add_fusion.3), channel_id=1, source_target_pairs={{0,128},{8,136},{16,144},{24,152},{32,160},{40,168},{48,176},{56,1... | collective-permute-start | bytes 786440 | tf_op jit(solution)/shard_map/ppermute | solution.py:16
  213.8 19.2 %collective-permute-start.12 = (f32[4,128,128]{2,1,0:T(8,128)S(1)}, f32[4,128,128]{2,1,0:T(8,128)S(1)}, u32[]{:S(2)}, u32[]{:S(2)}) collective-permute-start(f32[4,128,128]{2,1,0:T(8,128)S(1)} %convolution_add_fusion.2), channel_id=1, source_target_pairs={{0,8},{8,16},{16,24},{24,32},{32,40},{40,48},{48,56},{56,64},{64,7... | collective-permute-start | bytes 786440 | tf_op jit(solution)/shard_map/ppermute | solution.py:16
  233.1 21.5 %copy-start.1 = (f32[8,4,64,128]{3,2,1,0:T(8,128)S(1)}, f32[8,4,64,128]{3,2,1,0:T(8,128)}, u32[]{:S(2)}) copy-start(f32[8,4,64,128]{3,2,1,0:T(8,128)} %get-tuple-element.282) | copy-start | bytes 3145732
  254.9 1.5 copy-start.6
